TPU v7x, 128 devices: a whole 4x4x4 slice. The times are simulated.
128 devices in a mesh: batch: 16 (over z_lo, x, core), patch: 8 (over z_hi, y).
Axes of the slice: x: 4, y: 4, z: 4 (z_hi: 2, z_lo: 2; z = z_hi * 2 + z_lo), core: 2. Of those that a mesh axis runs over, the one named last changes fastest.
Arguments:
- hidden_in: bfloat16 [49152, 1280], P(('batch', 'patch')), parts along dimension 0, may hold values from -45 to 45
- stale_keys: bfloat16 [49152, 1280], P(('batch', 'patch')), parts along dimension 0, may hold values from -150 to 150
- stale_values: bfloat16 [49152, 1280], P(('batch', 'patch')), parts along dimension 0, may hold values from -12 to 12
- stale_moments: float32 [768, 2, 2, 32], P(('batch', 'patch')), parts along dimension 0, may hold values from -5120 to 102400, as said below
- gain_attn: float32 [1280], replicated, may hold values from 0.1 to 1.9
- bias_attn: float32 [1280], replicated, may hold values from -3 to 3
- w_query: bfloat16 [1280, 1280], replicated, may hold values from -0.3125 to 0.3125
- w_key: bfloat16 [1280, 1280], replicated, may hold values from -0.625 to 0.625
- w_value: bfloat16 [1280, 1280], replicated, may hold values from -0.625 to 0.625
- gain_conv: float32 [1280], replicated, may hold values from 0.1 to 1.9
- bias_conv: float32 [1280], replicated, may hold values from -3 to 3
- conv_weight: bfloat16 [3, 3, 1280, 640], replicated, may hold values from -0.0546875 to 0.0546875
- conv_bias: float32 [640], replicated, may hold values from -3 to 3
- w_time: bfloat16 [320, 640], replicated, may hold values from -0.3125 to 0.3125
- timestep: int32 [1], replicated, may hold values from 0 to 999
Outputs:
- conv_out: bfloat16 [49152, 640], P(('batch', 'patch')), parts along dimension 0
There are 16 independent parts, one for each index of `batch`. A program takes and returns all parts, laid end to end along the dimension named above; an argument that names none is the same for every part. Nothing has to cross between parts.
Inputs may be any that keep to these rules, and one draw needn't show every extreme that they name: `stale_moments`: each row's entries are the sums and sums of squares of 2560 values: that count times the second is at least the square of the first.
All inputs are finite; a program needn't handle non-finite values.
Results may differ from a plain program's by a relative error of at most 0.008.
The roundings to bfloat16 on the way count: a program that leaves them out, or rounds other values in their place, can miss the bound.
Values may be sent and summed in bfloat16 or wider, within the bound.
No kernel may reach another device: no remote copies, remote signals or barrier semaphores. Data moves between devices by JAX's collectives and lax.ppermute only.
A program may use at most 320 MiB of HBM per device.

v0:
```python
import math

import jax
import jax.numpy as jnp
from jax import lax
from jax.sharding import PartitionSpec as P

HEADS = 20
GROUPS = 32
W = 64


EPS = 1e-05
NEG = -1e30


def padded_2(cells, sides, width):
    for axis, dim in sides:
        count = lax.axis_size(axis)
        ends = count - 1
        head = lax.slice_in_dim(cells, 0, width, axis=dim)
        tail = lax.slice_in_dim(cells, cells.shape[dim] - width, cells.shape[dim], axis=dim)
        cells = jnp.concatenate(
            [
                lax.ppermute(tail, axis, [(i, (i + 1) % count) for i in range(ends)]),
                cells,
                lax.ppermute(head, axis, [((i + 1) % count, i) for i in range(ends)]),
            ],
            axis=dim,
        )
    return cells


def group_moments(rows_in, groups):
    values = rows_in.astype(jnp.float32).reshape(
        rows_in.shape[0], groups, rows_in.shape[1] // groups
    )
    return jnp.stack([jnp.sum(values, axis=(0, 2)), jnp.sum(values * values, axis=(0, 2))])


def group_normalize(rows_in, totals, count, gain, offset, groups):
    average = totals[0] / count
    variance = totals[1] / count - average * average
    inverse = lax.rsqrt(variance + EPS)
    group_width = rows_in.shape[1] // groups
    factors = jnp.repeat(inverse, group_width) * gain
    shifts = offset - jnp.repeat(average * inverse, group_width) * gain
    return rows_in.astype(jnp.float32) * factors + shifts


def time_embedding(timestep, w_time):
    half_dim = w_time.shape[0] // 2
    frequency = jnp.exp(-math.log(10000.0) * jnp.arange(half_dim, dtype=jnp.float32) / half_dim)
    angles = timestep[0].astype(jnp.float32) * frequency
    embedded = jnp.concatenate([jnp.cos(angles), jnp.sin(angles)])
    return jnp.dot(embedded[None, :], w_time.astype(jnp.float32), precision=lax.Precision.HIGHEST)[
        0
    ]


def body(
    hidden_in,
    stale_keys,
    stale_values,
    stale_moments,
    gain_attn,
    bias_attn,
    w_query,
    w_key,
    w_value,
    gain_conv,
    bias_conv,
    conv_weight,
    conv_bias,
    w_time,
    timestep,
):
    devices = lax.axis_size("patch")
    position = lax.axis_index("patch")
    tok_rows = hidden_in.shape[0]
    channels = hidden_in.shape[1]
    head_dim = channels // HEADS
    all_tokens = tok_rows * devices
    count = all_tokens * (channels // GROUPS)
    scale_qk = head_dim ** (-0.5)
    own_first = position * tok_rows
    own_stale = jnp.sum(stale_moments, axis=0)
    total_attn = lax.psum(own_stale[0], "patch")
    totals_attn = total_attn - own_stale[0] + group_moments(hidden_in, GROUPS)
    normed = group_normalize(hidden_in, totals_attn, count, gain_attn, bias_attn, GROUPS).astype(
        jnp.bfloat16
    )
    query = jnp.dot(normed, w_query, preferred_element_type=jnp.float32).astype(jnp.bfloat16)
    key_fresh = jnp.dot(normed, w_key, preferred_element_type=jnp.float32).astype(jnp.bfloat16)
    value_fresh = jnp.dot(normed, w_value, preferred_element_type=jnp.float32).astype(jnp.bfloat16)
    query3 = query.reshape(tok_rows, HEADS, head_dim)
    key3 = key_fresh.reshape(tok_rows, HEADS, head_dim)
    value3 = value_fresh.reshape(tok_rows, HEADS, head_dim)
    fresh_scores = (
        jnp.einsum("qhd,khd->qhk", query3, key3, preferred_element_type=jnp.float32) * scale_qk
    )
    start_max = jnp.max(fresh_scores, axis=-1)
    fresh_weights = jnp.exp(fresh_scores - start_max[..., None])
    start_sum = jnp.sum(fresh_weights, axis=-1)
    start_acc = jnp.einsum(
        "qhk,khd->qhd",
        fresh_weights.astype(jnp.bfloat16),
        value3,
        preferred_element_type=jnp.float32,
    )
    keys_piece = lax.all_gather(stale_keys, "patch", axis=0, tiled=True)
    values_piece = lax.all_gather(stale_values, "patch", axis=0, tiled=True)
    key_count = keys_piece.shape[0]
    scores = (
        jnp.einsum(
            "qhd,khd->qhk",
            query3,
            keys_piece.reshape(key_count, HEADS, head_dim),
            preferred_element_type=jnp.float32,
        )
        * scale_qk
    )
    key_index = jnp.arange(key_count, dtype=jnp.int32)
    own_keys = (key_index >= own_first) & (key_index < own_first + tok_rows)
    scores = jnp.where(own_keys[None, None, :], NEG, scores)
    max_new = jnp.maximum(start_max, jnp.max(scores, axis=-1))
    rescale_old = jnp.exp(start_max - max_new)
    weights = jnp.exp(scores - max_new[..., None])
    sum_new = start_sum * rescale_old + jnp.sum(weights, axis=-1)
    acc_new = start_acc * rescale_old[..., None] + jnp.einsum(
        "qhk,khd->qhd",
        weights.astype(jnp.bfloat16),
        values_piece.reshape(key_count, HEADS, head_dim),
        preferred_element_type=jnp.float32,
    )
    attended = (acc_new / sum_new[..., None]).reshape(tok_rows, channels)
    updated = (hidden_in.astype(jnp.float32) + attended).astype(jnp.bfloat16)
    total_conv = lax.psum(own_stale[1], "patch")
    totals_conv = total_conv - own_stale[1] + group_moments(updated, GROUPS)
    normed_conv = group_normalize(updated, totals_conv, count, gain_conv, bias_conv, GROUPS)
    activated = jax.nn.silu(normed_conv).astype(jnp.bfloat16).reshape(tok_rows // W, W, channels)
    padded = padded_2(activated, (("patch", 0),), 1)
    convolved = lax.conv_general_dilated(
        padded[None],
        conv_weight,
        (1, 1),
        ((0, 0), (1, 1)),
        dimension_numbers=("NHWC", "HWIO", "NHWC"),
        preferred_element_type=jnp.float32,
    )[0]
    temb = time_embedding(timestep, w_time)
    conv_out = (convolved + conv_bias + temb).astype(jnp.bfloat16)
    return conv_out.reshape(tok_rows, conv_weight.shape[3])


def solution(mesh):
    return jax.shard_map(
        body,
        mesh=mesh,
        in_specs=(
            P(("batch", "patch"), None),
            P(("batch", "patch"), None),
            P(("batch", "patch"), None),
            P(("batch", "patch"), None, None, None),
            P(),
            P(),
            P(),
            P(),
            P(),
            P(),
            P(),
            P(),
            P(),
            P(),
            P(),
        ),
        out_specs=P(("batch", "patch"), None),
        check_vma=False,
    )
```

profile of v0, /device:TPU:64, one launch (start us, length us, event | category | flops | bytes accessed | tf_op | source)
XLA Modules:
  0.0 319.2 jit_solution(11762423095533012177)
XLA Ops:
  6.5 0.7 all-gather.3.cloned.1.call-update
  7.3 0.0 all-gather.5.cloned.1.call-start
  7.3 0.7 all-gather.5.cloned.1.call-update
  8.0 1.5 convert_reduce_fusion
  9.5 0.1 reduce_sum.96
  9.6 0.1 reduce_sum.75
  9.7 0.1 reduce_sum.97
  9.8 0.1 reduce_sum.76
  9.9 0.7 reduce_sum.73
  10.6 21.3 %all-reduce = (f32[2,32]{1,0:T(2,128)S(1)}, f32[2,32]{1,0:T(2,128)S(1)}) all-reduce(f32[2,32]{1,0:T(2,128)S(1)} %get-tuple-element.25, f32[2,32]{1,0:T(2,128)S(1)} %get-tuple-element.24), channel_id=1, replica_groups=mesh['batch'=16,'patch'=8] {'patch'}, use_global_device_ids=true, to_apply=%region_1.0 | all-reduce | flops 128 | bytes 1024 | tf_op jit(solution)/shard_map/psum | solution.py:88
  31.9 0.1 broadcast_in_dim.22
  32.0 0.1 reshape.91
  32.1 0.1 broadcast_in_dim.23
  32.2 0.1 reshape.92
  32.3 0.7 fusion.64
  33.0 3.7 %convolution_convert_fusion = bf16[384,1280]{1,0:T(8,128)(2,1)} fusion(bf16[1280,1280]{1,0:T(8,128)(2,1)S(1)} %copy-done, bf16[384,1280]{1,0:T(8,128)(2,1)} %param.15, f32[1280]{0:T(1024)S(1)} %get-tuple-element.23, f32[1280]{0:T(1024)S(1)} %get-tuple-element.22), kind=kOutput, calls=%fused_computation.25 | convolution fusion | flops 1260748800 | bytes 5253120 | tf_op jit(solution)/shard_map/dot_general | solution.py:93
  36.7 1.6 copy.52
  38.3 4.8 %convolution_convert_fusion.1 = bf16[384,1280]{1,0:T(8,128)(2,1)} fusion(bf16[1280,1280]{1,0:T(8,128)(2,1)} %param.22, bf16[384,1280]{1,0:T(8,128)(2,1)} %param.15, f32[1280]{0:T(1024)S(1)} %get-tuple-element.23, f32[1280]{0:T(1024)S(1)} %get-tuple-element.22), kind=kOutput, calls=%fused_computation.26 | convolution fusion | flops 1260748800 | bytes 5253120 | tf_op jit(solution)/shard_map/dot_general | solution.py:94
  43.1 1.6 copy.51
  44.7 4.4 %convolution_convert_fusion.2 = bf16[384,1280]{1,0:T(8,128)(2,1)} fusion(bf16[1280,1280]{1,0:T(8,128)(2,1)} %param.23, bf16[384,1280]{1,0:T(8,128)(2,1)S(1)} %copy-done.3, f32[1280]{0:T(1024)S(1)} %get-tuple-element.23, f32[1280]{0:T(1024)S(1)} %get-tuple-element.22), kind=kOutput, calls=%fused_computation.27 | convolution fusion | flops 1260748800 | bytes 5253120 | tf_op jit(solution)/shard_map/dot_general | solution.py:95
  49.1 2.3 copy.50
  52.1 1.7 bitcast_reduce_fusion.1
  53.8 4.2 %copy-done.2 = f32[20,384,384]{2,1,0:T(8,128)} copy-done((f32[20,384,384]{2,1,0:T(8,128)}, f32[20,384,384]{2,1,0:T(8,128)S(1)}, u32[]{:S(2)}) %copy-start.2) | copy-done | bytes 11796504
  58.1 2.0 fusion.7
  60.0 52.3 %all-gather.3.cloned.1.call-done = bf16[3072,1280]{1,0:T(8,128)(2,1)} async-done(((bf16[384,1280]{1,0:T(8,128)(2,1)}), bf16[3072,1280]{1,0:T(8,128)(2,1)}) %all-gather.3.cloned.1.call-update) | async-done | bytes 7864336 | tf_op jit(solution)/shard_map/all_gather | solution.py:111
  112.3 10.6 %copy.54 = bf16[3072,1280]{0,1:T(8,128)(2,1)} copy(bf16[3072,1280]{1,0:T(8,128)(2,1)} %all-gather.3.cloned.1.call-done) | data formatting | bytes 15728640 | tf_op jit(solution)/shard_map/all_gather | solution.py:111
  122.9 36.3 %bitcast_reduce_fusion = (f32[384,20]{0,1:T(8,128)S(1)}, f32[20,384,3072]{2,1,0:T(8,128)}) fusion(pred[3072]{0:T(1024)(128)(4,1)S(1)} %fusion.45, bf16[384,20,64]{0,2,1:T(8,128)(2,1)S(1)} %bitcast.113, bf16[3072,20,64]{0,2,1:T(8,128)(2,1)} %bitcast.111), kind=kOutput, calls=%fused_computation.1 | convolution fusion | flops 3090670080 | bytes 103252992 | tf_op jit(solution)/shard_map/qhd,khd->qhk/dot_general | solution.py:115
  159.3 29.4 %fusion.1 = f32[384,20]{0,1:T(8,128)S(1)} fusion(f32[20,384,3072]{2,1,0:T(8,128)} %get-tuple-element.29, f32[384,20]{0,1:T(8,128)S(1)} %max.13, pred[3072]{0:T(1024)(128)(4,1)S(1)} %fusion.45), kind=kLoop, calls=%fused_computation.4 | loop fusion | flops 94364160 | bytes 94436352 | tf_op jit(solution)/shard_map/reduce_sum | solution.py:129
  188.7 27.3 %all-gather.5.cloned.1.call-done = bf16[3072,1280]{1,0:T(8,128)(2,1)} async-done(((bf16[384,1280]{1,0:T(8,128)(2,1)}), bf16[3072,1280]{1,0:T(8,128)(2,1)}) %all-gather.5.cloned.1.call-update) | async-done | bytes 7864336 | tf_op jit(solution)/shard_map/all_gather | solution.py:112
  216.0 10.6 %copy.55 = bf16[3072,1280]{0,1:T(8,128)(2,1)} copy(bf16[3072,1280]{1,0:T(8,128)(2,1)} %all-gather.5.cloned.1.call-done) | data formatting | bytes 15728640 | tf_op jit(solution)/shard_map/all_gather | solution.py:112
  226.6 35.4 %fusion.3 = f32[20,384,64]{1,2,0:T(8,128)} fusion(bf16[3072,20,64]{0,2,1:T(8,128)(2,1)} %bitcast.114, f32[20,384,3072]{2,1,0:T(8,128)} %get-tuple-element.29, f32[384,20]{0,1:T(8,128)S(1)} %max.13, pred[3072]{0:T(1024)(128)(4,1)S(1)} %fusion.45), kind=kOutput, calls=%fused_computation.6 | convolution fusion | flops 3114270720 | bytes 104236032 | tf_op jit(solution)/shard_map/qhk,khd->qhd/dot_general | solution.py:130
  262.0 8.6 %fusion.26 = f32[384,20,64]{0,2,1:T(8,128)} fusion(f32[20,384,64]{1,2,0:T(8,128)} %fusion.3, bf16[384,20,64]{0,2,1:T(8,128)(2,1)S(1)} %bitcast.120, f32[20,384,384]{2,1,0:T(8,128)} %copy-done.2, f32[384,20]{0,1:T(8,128)S(1)} %get-tuple-element.26, f32[384,20]{0,1:T(8,128)S(1)} %get-tuple-element.14, f32[384,20]{0,1:T(8,128)S(1)} %get-tuple-element.15), kind=kOutput, calls=%fused_computation.41 | convolution fusion | flops 387809280 | bytes 16803840 | tf_op jit(solution)/shard_map/qhk,khd->qhd/dot_general | solution.py:105
  270.6 1.9 copy.56
  272.5 1.3 convert_reduce_fusion.1
  273.8 0.1 reduce_sum.104
  273.9 0.1 reduce_sum.105
  274.0 0.1 reduce_sum.101
  274.1 0.1 reduce_sum.102
  274.2 0.1 broadcast_in_dim.42
  274.3 0.1 reshape.99
  274.4 0.1 broadcast_in_dim.43
  274.5 0.1 reshape.100
  274.6 1.8 fusion.21
  276.4 5.3 %collective-permute-start.1 = (bf16[1,64,1280]{2,1,0:T(8,128)(2,1)S(1)}, bf16[1,64,1280]{2,1,0:T(8,128)(2,1)S(1)}, u32[]{:S(2)}, u32[]{:S(2)}) collective-permute-start(bf16[1,64,1280]{2,1,0:T(8,128)(2,1)S(1)} %get-tuple-element.19), channel_id=1, source_target_pairs={{1,0},{2,1},{3,2},{4,3},{5,4},{6,5},{7,6},{9,8},{10,9},{11,10},{12... | collective-permute-start | bytes 491528 | tf_op jit(solution)/shard_map/ppermute | solution.py:27
  281.7 1.9 collective-permute-start
  283.7 0.1 pad_maximum_fusion
  283.8 1.3 convolution_reduce_fusion
  285.0 0.6 copy.58
  285.6 0.3 copy.59
  285.9 6.7 %collective-permute-done = bf16[1,64,1280]{2,1,0:T(8,128)(2,1)S(1)} collective-permute-done((bf16[1,64,1280]{2,1,0:T(8,128)(2,1)S(1)}, bf16[1,64,1280]{2,1,0:T(8,128)(2,1)S(1)}, u32[]{:S(2)}, u32[]{:S(2)}) %collective-permute-start) | collective-permute-done | bytes 163872 | tf_op jit(solution)/shard_map/ppermute | solution.py:25
  292.6 0.3 copy.57
  292.8 1.1 maximum_bitcast_fusion
  293.9 0.0 copy-start.8
  293.9 0.1 pad
  294.0 0.2 copy.61
  294.3 0.1 slice.48
  294.4 0.2 copy-done.8
  294.6 15.6 %fusion.36 = f32[6,8,9,640]{3,1,2,0:T(8,128)S(1)} fusion(bf16[3,3,1280,640]{3,2,1,0:T(8,128)(2,1)} %param.26, bf16[8,1,7,2,1280]{4,2,3,0,1:T(8,128)(2,1)S(1)} %slice.48, bf16[8,1,8,9,1280]{4,2,3,0,1:T(8,128)(2,1)S(1)} %copy.61, pred[8,9]{0,1:T(8,128)(4,1)S(1)} %copy-done.8), kind=kOutput, calls=%fused_computation.49 | convolution fusion | flops 6375782400 | bytes 17612872 | tf_op jit(solution)/shard_map/conv_general_dilated | solution.py:143
  310.2 0.3 copy.62
  310.5 0.1 slice.49
  310.6 0.2 copy.63
  310.8 0.1 copy-done.7
  310.9 0.9 fusion.40
  311.8 0.6 copy-done.1
  (27 shorter events, 0.2 us)
Async XLA Ops:
  6.5 26.5 %copy-start = (bf16[1280,1280]{1,0:T(8,128)(2,1)S(1)}, bf16[1280,1280]{1,0:T(8,128)(2,1)}, u32[]{:S(2)}) copy-start(bf16[1280,1280]{1,0:T(8,128)(2,1)} %param.21) | copy-start | bytes 9830404
  6.5 105.8 %all-gather.3.cloned.1.call-start = ((), (), s32[]{:S(2)}) async-start(), calls=%async_computation | async-start | bytes 8847360 | tf_op jit(solution)/shard_map/all_gather | solution.py:111
  7.3 208.8 %all-gather.5.cloned.1.call-start = ((), (), s32[]{:S(2)}) async-start(), calls=%async_computation.1 | async-start | bytes 8847360 | tf_op jit(solution)/shard_map/all_gather | solution.py:112
  38.3 6.4 %copy-start.3 = (bf16[384,1280]{1,0:T(8,128)(2,1)S(1)}, bf16[384,1280]{1,0:T(8,128)(2,1)}, u32[]{:S(2)}) copy-start(bf16[384,1280]{1,0:T(8,128)(2,1)} %param.15) | copy-start | bytes 2949124
  53.8 4.3 %copy-start.2 = (f32[20,384,384]{2,1,0:T(8,128)}, f32[20,384,384]{2,1,0:T(8,128)S(1)}, u32[]{:S(2)}) copy-start(f32[20,384,384]{2,1,0:T(8,128)S(1)} %get-tuple-element.27) | copy-start | bytes 35389444
  226.6 35.4 %copy-start.4 = (bf16[384,1280]{0,1:T(8,128)(2,1)S(1)}, bf16[384,1280]{0,1:T(8,128)(2,1)}, u32[]{:S(2)}) copy-start(bf16[384,1280]{0,1:T(8,128)(2,1)} %copy.50) | copy-start | bytes 2949124
  270.6 4.0 %copy-start.5 = (f32[1280]{0:T(1024)S(1)}, f32[1280]{0:T(1024)}, u32[]{:S(2)}) copy-start(f32[1280]{0:T(1024)} %param.24) | copy-start | bytes 15364
  270.6 4.0 %copy-start.6 = (f32[1280]{0:T(1024)S(1)}, f32[1280]{0:T(1024)}, u32[]{:S(2)}) copy-start(f32[1280]{0:T(1024)} %param.25) | copy-start | bytes 15364
  276.4 9.2 %collective-permute-start.1 = (bf16[1,64,1280]{2,1,0:T(8,128)(2,1)S(1)}, bf16[1,64,1280]{2,1,0:T(8,128)(2,1)S(1)}, u32[]{:S(2)}, u32[]{:S(2)}) collective-permute-start(bf16[1,64,1280]{2,1,0:T(8,128)(2,1)S(1)} %get-tuple-element.19), channel_id=1, source_target_pairs={{1,0},{2,1},{3,2},{4,3},{5,4},{6,5},{7,6},{9,8},{10,9},{11,10},{12... | collective-permute-start | bytes 491528 | tf_op jit(solution)/shard_map/ppermute | solution.py:27
  281.7 10.8 %collective-permute-start = (bf16[1,64,1280]{2,1,0:T(8,128)(2,1)S(1)}, bf16[1,64,1280]{2,1,0:T(8,128)(2,1)S(1)}, u32[]{:S(2)}, u32[]{:S(2)}) collective-permute-start(bf16[1,64,1280]{2,1,0:T(8,128)(2,1)S(1)} %get-tuple-element.18), channel_id=1, source_target_pairs={{0,1},{1,2},{2,3},{3,4},{4,5},{5,6},{6,7},{8,9},{9,10},{10,11},{11... | collective-permute-start | bytes 491528 | tf_op jit(solution)/shard_map/ppermute | solution.py:25
  293.9 0.7 copy-start.8
  310.2 0.7 copy-start.7
  310.2 2.1 copy-start.1
Sparse Core Ops, SparseCore 0:
  9.7 102.6 all-gather.2
  114.7 101.3 all-gather.4
where the time goes:
time: 320 us; the launch traced here: 319 us
  matrix products  112 us (35%)
  waiting for transfers between devices  87.7 us (27%)
  other arithmetic  40 us (12%)
  local copies, waits for them, and re-layouts  36.7 us (11%)
  blocking collectives  21.3 us (7%)
  between operations  14.4 us (4%)
  starting transfers between devices  7.29 us (2%)
    all_gather x1, waiting for transfers between devices, body(): keys_piece = lax.all_gather(stale_keys, 'patch', axis=0, tiled=True)  52.3 us
    dot_general x1, matrix products, body(): jnp.einsum('qhd,khd->qhk', query3, keys_piece.reshape(key_count, HEADS, h...  36.3 us
    dot_general x1, matrix products, body(): jnp.einsum('qhk,khd->qhd', weights.astype(jnp.bfloat16), values_piece.res...  35.4 us
    reduce_sum x1, other arithmetic, body(): sum_new = start_sum * rescale_old + jnp.sum(weights, axis=-1)  29.4 us
    all_gather x1, waiting for transfers between devices, body(): values_piece = lax.all_gather(stale_values, 'patch', axis=0, tiled=True)  27.3 us
    psum x1, blocking collectives, body(): total_attn = lax.psum(own_stale[0], 'patch')  21.3 us
    conv_general_dilated x1, matrix products, body(): lax.conv_general_dilated(padded[None], conv_weight, (1, 1), ((0, 0), (1,...  15.6 us
    all_gather x1, local copies, waits for them, and re-layouts, body(): values_piece = lax.all_gather(stale_values, 'patch', axis=0, tiled=True)  10.6 us
  transfers between devices with their start and end apart: 4, of which 3 were waited for; matrix products, arithmetic and copies ran while one was open for 33% of the time, Pallas kernels for 0%

commit v1 on v0

--- a/solution.py
+++ b/solution.py
@@ -4,10 +4,14 @@
 import jax.numpy as jnp
 from jax import lax
 from jax.sharding import PartitionSpec as P
+from jax.experimental import pallas as pl
+from jax.experimental.pallas import tpu as pltpu
 
 HEADS = 20
 GROUPS = 32
 W = 64
+NCHUNK = 2
+QBLK = 128
 
 
 EPS = 1e-05
@@ -56,6 +60,48 @@
     return jnp.dot(embedded[None, :], w_time.astype(jnp.float32), precision=lax.Precision.HIGHEST)[
         0
     ]
+
+
+def attn_kernel(q_ref, k_ref, v_ref, h_ref, o_ref):
+    head_dim = q_ref.shape[1] // 2
+    scale = head_dim ** (-0.5)
+    for hh in range(2):
+        lanes = slice(hh * head_dim, (hh + 1) * head_dim)
+        kh = k_ref[:, lanes]
+        vh = v_ref[:, lanes]
+        for qb in range(q_ref.shape[0] // QBLK):
+            rows = slice(qb * QBLK, (qb + 1) * QBLK)
+            qh = q_ref[rows, lanes]
+            s = lax.dot_general(
+                qh, kh, (((1,), (1,)), ((), ())), preferred_element_type=jnp.float32
+            ) * scale
+            m = jnp.max(s, axis=1, keepdims=True)
+            w = jnp.exp(s - m)
+            total = jnp.sum(w, axis=1, keepdims=True)
+            acc = jnp.dot(w.astype(jnp.bfloat16), vh, preferred_element_type=jnp.float32)
+            att = acc / total
+            o_ref[rows, lanes] = (h_ref[rows, lanes].astype(jnp.float32) + att).astype(
+                jnp.bfloat16
+            )
+
+
+def attention_chunk(query, keys, values, hidden, chunk):
+    tok_rows, width = query.shape
+    key_count = keys.shape[0]
+    pairs = width // 128
+    return pl.pallas_call(
+        attn_kernel,
+        grid=(pairs,),
+        in_specs=[
+            pl.BlockSpec((tok_rows, 128), lambda h: (0, h)),
+            pl.BlockSpec((key_count, 128), lambda h: (0, h)),
+            pl.BlockSpec((key_count, 128), lambda h: (0, h)),
+            pl.BlockSpec((tok_rows, 128), lambda h: (0, h + chunk * pairs)),
+        ],
+        out_specs=pl.BlockSpec((tok_rows, 128), lambda h: (0, h)),
+        out_shape=jax.ShapeDtypeStruct((tok_rows, width), jnp.bfloat16),
+        compiler_params=pltpu.CompilerParams(vmem_limit_bytes=48 * 1024 * 1024),
+    )(query, keys, values, hidden)
 
 
 def body(
@@ -79,11 +125,19 @@
     position = lax.axis_index("patch")
     tok_rows = hidden_in.shape[0]
     channels = hidden_in.shape[1]
-    head_dim = channels // HEADS
     all_tokens = tok_rows * devices
     count = all_tokens * (channels // GROUPS)
-    scale_qk = head_dim ** (-0.5)
     own_first = position * tok_rows
+    width = channels // NCHUNK
+    gathered = []
+    for c in range(NCHUNK):
+        cols = slice(c * width, (c + 1) * width)
+        gathered.append(
+            (
+                lax.all_gather(stale_keys[:, cols], "patch", axis=0, tiled=True),
+                lax.all_gather(stale_values[:, cols], "patch", axis=0, tiled=True),
+            )
+        )
     own_stale = jnp.sum(stale_moments, axis=0)
     total_attn = lax.psum(own_stale[0], "patch")
     totals_attn = total_attn - own_stale[0] + group_moments(hidden_in, GROUPS)
@@ -93,48 +147,15 @@
     query = jnp.dot(normed, w_query, preferred_element_type=jnp.float32).astype(jnp.bfloat16)
     key_fresh = jnp.dot(normed, w_key, preferred_element_type=jnp.float32).astype(jnp.bfloat16)
     value_fresh = jnp.dot(normed, w_value, preferred_element_type=jnp.float32).astype(jnp.bfloat16)
-    query3 = query.reshape(tok_rows, HEADS, head_dim)
-    key3 = key_fresh.reshape(tok_rows, HEADS, head_dim)
-    value3 = value_fresh.reshape(tok_rows, HEADS, head_dim)
-    fresh_scores = (
-        jnp.einsum("qhd,khd->qhk", query3, key3, preferred_element_type=jnp.float32) * scale_qk
-    )
-    start_max = jnp.max(fresh_scores, axis=-1)
-    fresh_weights = jnp.exp(fresh_scores - start_max[..., None])
-    start_sum = jnp.sum(fresh_weights, axis=-1)
-    start_acc = jnp.einsum(
-        "qhk,khd->qhd",
-        fresh_weights.astype(jnp.bfloat16),
-        value3,
-        preferred_element_type=jnp.float32,
-    )
-    keys_piece = lax.all_gather(stale_keys, "patch", axis=0, tiled=True)
-    values_piece = lax.all_gather(stale_values, "patch", axis=0, tiled=True)
-    key_count = keys_piece.shape[0]
-    scores = (
-        jnp.einsum(
-            "qhd,khd->qhk",
-            query3,
-            keys_piece.reshape(key_count, HEADS, head_dim),
-            preferred_element_type=jnp.float32,
+    pieces = []
+    for c in range(NCHUNK):
+        cols = slice(c * width, (c + 1) * width)
+        keys_used = lax.dynamic_update_slice_in_dim(gathered[c][0], key_fresh[:, cols], own_first, 0)
+        values_used = lax.dynamic_update_slice_in_dim(
+            gathered[c][1], value_fresh[:, cols], own_first, 0
         )
-        * scale_qk
-    )
-    key_index = jnp.arange(key_count, dtype=jnp.int32)
-    own_keys = (key_index >= own_first) & (key_index < own_first + tok_rows)
-    scores = jnp.where(own_keys[None, None, :], NEG, scores)
-    max_new = jnp.maximum(start_max, jnp.max(scores, axis=-1))
-    rescale_old = jnp.exp(start_max - max_new)
-    weights = jnp.exp(scores - max_new[..., None])
-    sum_new = start_sum * rescale_old + jnp.sum(weights, axis=-1)
-    acc_new = start_acc * rescale_old[..., None] + jnp.einsum(
-        "qhk,khd->qhd",
-        weights.astype(jnp.bfloat16),
-        values_piece.reshape(key_count, HEADS, head_dim),
-        preferred_element_type=jnp.float32,
-    )
-    attended = (acc_new / sum_new[..., None]).reshape(tok_rows, channels)
-    updated = (hidden_in.astype(jnp.float32) + attended).astype(jnp.bfloat16)
+        pieces.append(attention_chunk(query[:, cols], keys_used, values_used, hidden_in, c))
+    updated = jnp.concatenate(pieces, axis=1)
     total_conv = lax.psum(own_stale[1], "patch")
     totals_conv = total_conv - own_stale[1] + group_moments(updated, GROUPS)
     normed_conv = group_normalize(updated, totals_conv, count, gain_conv, bias_conv, GROUPS)

time: 320 us -> 399 us (1.25); the launches traced: 319 us -> 394 us
  waiting for transfers between devices: 87.7 us -> 240 us
  matrix products: 112 us -> 24.6 us
  Pallas kernels: 0 us -> 49.2 us
  other arithmetic: 40 us -> 6.91 us
  local copies, waits for them, and re-layouts: 36.7 us -> 28.6 us
    all_gather x2 -> x4, waiting for transfers between devices: 79.6 us -> 237 us  [the longest x2 137 us: body(): lax.all_gather(stale_keys[:, cols], 'patch', axis=0, tiled=True)]
    dot_general x4 -> x0, matrix products: 82 us -> none  [the longest x1 36.3 us: body(): jnp.einsum('qhd,khd->qhk', query3, keys_piece.reshape(key_count, HEADS, h...]
    pallas_call x0 -> x2, Pallas kernels: none -> 49.2 us  [attention_chunk(): pl.pallas_call(attn_kernel, grid=(pairs,), in_specs=[pl.BlockSpec((tok_ro...]
    reduce_sum x2 -> x0, other arithmetic: 31.4 us -> none  [the longest x1 29.4 us: body(): sum_new = start_sum * rescale_old + jnp.sum(weights, axis=-1)]
    all_gather x2 -> x0, local copies, waits for them, and re-layouts: 21.2 us -> none  [the longest x1 10.6 us: body(): values_piece = lax.all_gather(stale_values, 'patch', axis=0, tiled=True)]
    ppermute x1, waiting for transfers between devices: 6.69 us -> 0.52 us  [padded_2(): lax.ppermute(tail, axis, [(i, (i + 1) % count) for i in range(ends)])]
    slice x0 -> x3, local copies, waits for them, and re-layouts: none -> 5.66 us  [the longest x1 2.38 us: body(): stale_values[:, cols]]
    convert_element_type x3 -> x0, local copies, waits for them, and re-layouts: 5.42 us -> none  [the longest x1 2.27 us: body(): jnp.dot(normed, w_value, preferred_element_type=jnp.float32)]
  transfers between devices with their start and end apart: 4 -> 6, of which waited for: 3 -> 6; matrix products, arithmetic and copies ran while one was open for 33% -> 5% of each run, Pallas kernels for 0% -> 0%
where the time goes in v1:
time: 399 us; the launch traced here: 394 us
  waiting for transfers between devices  240 us (60%)
  Pallas kernels  49.2 us (12%)
  local copies, waits for them, and re-layouts  28.6 us (7%)
  matrix products  24.6 us (6%)
  blocking collectives  21.2 us (5%)
  between operations  14.2 us (4%)
  starting transfers between devices  9.58 us (2%)
  other arithmetic  6.91 us (2%)
    all_gather x2, waiting for transfers between devices, body(): lax.all_gather(stale_keys[:, cols], 'patch', axis=0, tiled=True)  137 us
    all_gather x2, waiting for transfers between devices, body(): lax.all_gather(stale_values[:, cols], 'patch', axis=0, tiled=True)  100 us
    pallas_call x2, Pallas kernels, attention_chunk(): pl.pallas_call(attn_kernel, grid=(pairs,), in_specs=[pl.BlockSpec((tok_ro...  49.2 us
    psum x1, blocking collectives, body(): total_attn = lax.psum(own_stale[0], 'patch')  21.2 us
    conv_general_dilated x1, matrix products, body(): lax.conv_general_dilated(padded[None], conv_weight, (1, 1), ((0, 0), (1,...  15.6 us
    unnamed x42, local copies, waits for them, and re-layouts  9.27 us
  transfers between devices with their start and end apart: 6, of which 6 were waited for; matrix products, arithmetic and copies ran while one was open for 5% of the time, Pallas kernels for 0%

profile of v1, /device:TPU:64, one launch (start us, length us, event | category | flops | bytes accessed | tf_op | source)
XLA Modules:
  0.0 394.1 jit_solution(115696030790196764)
XLA Ops:
  6.5 2.4 fusion.34
  9.0 0.7 all-gather.7.cloned.1.call-update
  9.8 2.2 fusion.35
  12.0 0.0 all-gather.9.cloned.1.call-start
  12.1 0.5 all-gather.9.cloned.1.call-update
  12.6 1.5 convert_reduce_fusion
  14.1 0.1 reduce_sum.61
  14.2 0.1 reduce_sum.62
  14.3 0.1 reduce_sum.64
  14.4 0.1 reduce_sum.65
  14.5 21.2 %all-reduce = (f32[2,32]{1,0:T(2,128)S(1)}, f32[2,32]{1,0:T(2,128)S(1)}) all-reduce(f32[2,32]{1,0:T(2,128)S(1)} %get-tuple-element.32, f32[2,32]{1,0:T(2,128)S(1)} %get-tuple-element.31), channel_id=1, replica_groups=mesh['batch'=16,'patch'=8] {'patch'}, use_global_device_ids=true, to_apply=%region_1.0 | all-reduce | flops 128 | bytes 1024 | tf_op jit(solution)/shard_map/psum | solution.py:142
  35.7 0.1 broadcast_in_dim.10
  35.8 0.1 reshape.52
  35.9 0.1 broadcast_in_dim.22
  36.0 0.1 reshape.53
  36.8 0.1 pad_maximum_fusion.1
  36.9 1.3 convolution_reduce_fusion
  38.2 2.8 convolution_convert_fusion.2
  41.0 1.1 fusion.36
  42.1 0.5 copy-done.1
  42.6 2.4 convolution_convert_fusion
  45.0 2.4 convolution_convert_fusion.1
  47.5 30.7 %all-gather.11.cloned.1.call-done = bf16[3072,640]{1,0:T(8,128)(2,1)} async-done(((bf16[384,640]{1,0:T(8,128)(2,1)}), bf16[3072,640]{1,0:T(8,128)(2,1)}) %all-gather.11.cloned.1.call-update) | async-done | bytes 3932176 | tf_op jit(solution)/shard_map/all_gather | solution.py:138
  78.2 69.5 %all-gather.7.cloned.1.call-done = bf16[3072,640]{1,0:T(8,128)(2,1)} async-done(((bf16[384,640]{1,0:T(8,128)(2,1)}), bf16[3072,640]{1,0:T(8,128)(2,1)}) %all-gather.7.cloned.1.call-update) | async-done | bytes 3932176 | tf_op jit(solution)/shard_map/all_gather | solution.py:138
  147.7 2.2 slice_dynamic-update-slice_fusion.2
  149.9 67.3 %all-gather.5.cloned.1.call-done = bf16[3072,640]{1,0:T(8,128)(2,1)} async-done(((bf16[384,640]{1,0:T(8,128)(2,1)}), bf16[3072,640]{1,0:T(8,128)(2,1)}) %all-gather.5.cloned.1.call-update) | async-done | bytes 3932176 | tf_op jit(solution)/shard_map/all_gather | solution.py:137
  217.2 69.4 %all-gather.9.cloned.1.call-done = bf16[3072,640]{1,0:T(8,128)(2,1)} async-done(((bf16[384,640]{1,0:T(8,128)(2,1)}), bf16[3072,640]{1,0:T(8,128)(2,1)}) %all-gather.9.cloned.1.call-update) | async-done | bytes 3932176 | tf_op jit(solution)/shard_map/all_gather | solution.py:137
  286.6 2.3 slice_dynamic-update-slice_fusion.3
  288.9 2.1 copy-done.8
  291.0 24.6 %shard_map.145 = bf16[384,640]{1,0:T(8,128)(2,1)S(1)} custom-call(bf16[384,640]{1,0:T(8,128)(2,1)S(1)} %copy-done.11, bf16[3072,640]{1,0:T(8,128)(2,1)S(1)} %copy-done.8, bf16[3072,640]{1,0:T(8,128)(2,1)} %get-tuple-element.17.v_ref, bf16[384,1280]{1,0:T(8,128)(2,1)S(1)} %copy-done.2), custom_call_target="tpu_custom_call" | custom-call | tf_op jit(solution)/shard_map/pallas_call | solution.py:92
  315.6 0.8 copy-done.4
  316.4 2.0 copy.35
  318.4 1.2 copy-done.3
  319.6 2.1 copy-done.9
  321.7 1.0 copy-done.10
  322.7 24.6 %shard_map.146 = bf16[384,640]{1,0:T(8,128)(2,1)S(1)} custom-call(bf16[384,640]{1,0:T(8,128)(2,1)S(1)} %copy-done.10, bf16[3072,640]{1,0:T(8,128)(2,1)S(1)} %copy-done.9, bf16[3072,640]{1,0:T(8,128)(2,1)} %get-tuple-element.18.v_ref, bf16[384,1280]{1,0:T(8,128)(2,1)S(1)} %copy-done.3), custom_call_target="tpu_custom_call" | custom-call | tf_op jit(solution)/shard_map/pallas_call | solution.py:92
  347.4 0.8 copy-done.6
  348.2 2.1 copy.36
  350.2 1.7 convert_reduce_fusion.1
  351.9 0.1 broadcast_in_dim.23
  352.0 0.1 reshape.54
  352.1 0.1 broadcast_in_dim.24
  352.1 0.1 reshape.55
  352.3 1.4 copy.37
  353.7 1.3 copy.38
  355.0 0.6 multiply_convert_fusion.1
  355.6 2.2 collective-permute-start
  357.8 7.3 %collective-permute-start.1 = (bf16[1,64,1280]{2,1,0:T(8,128)(2,1)S(1)}, bf16[1,64,1280]{2,1,0:T(8,128)(2,1)S(1)}, u32[]{:S(2)}, u32[]{:S(2)}) collective-permute-start(bf16[1,64,1280]{2,1,0:T(8,128)(2,1)S(1)} %get-tuple-element.16), channel_id=1, source_target_pairs={{1,0},{2,1},{3,2},{4,3},{5,4},{6,5},{7,6},{9,8},{10,9},{11,10},{12... | collective-permute-start | bytes 491528 | tf_op jit(solution)/shard_map/ppermute | solution.py:31
  365.1 0.8 multiply_convert_fusion
  365.9 0.5 collective-permute-done
  366.5 0.3 copy.39
  366.7 1.2 collective-permute-done.1
  367.9 0.3 copy.40
  368.2 1.1 maximum_bitcast_fusion
  369.2 0.1 pad
  369.4 0.2 copy.42
  369.6 0.1 slice.94
  369.7 0.3 copy-done.20
  370.0 15.6 %fusion.12 = f32[6,8,9,640]{3,1,2,0:T(8,128)S(1)} fusion(bf16[3,3,1280,640]{3,2,1,0:T(8,128)(2,1)} %param.26, bf16[8,1,7,2,1280]{4,2,3,0,1:T(8,128)(2,1)S(1)} %slice.94, bf16[8,1,8,9,1280]{4,2,3,0,1:T(8,128)(2,1)S(1)} %copy.42, pred[8,9]{0,1:T(8,128)(4,1)S(1)} %copy-done.20), kind=kOutput, calls=%fused_computation.22 | convolution fusion | flops 6375782400 | bytes 17612872 | tf_op jit(solution)/shard_map/conv_general_dilated | solution.py:164
  385.7 0.3 copy.43
  386.0 0.1 slice.95
  386.1 0.2 copy.44
  386.3 0.4 copy-done.17
  386.7 0.9 fusion.16
  (49 shorter events, 0.4 us)
Async XLA Ops:
  6.5 31.7 %copy-start = (bf16[1280,1280]{1,0:T(8,128)(2,1)S(1)}, bf16[1280,1280]{1,0:T(8,128)(2,1)}, u32[]{:S(2)}) copy-start(bf16[1280,1280]{1,0:T(8,128)(2,1)} %param.21) | copy-start | bytes 9830404
  6.5 71.6 %all-gather.11.cloned.1.call-start = ((), (), s32[]{:S(2)}) async-start(), calls=%async_computation.3 | async-start | bytes 4423680 | tf_op jit(solution)/shard_map/all_gather | solution.py:138
  8.9 138.7 %all-gather.7.cloned.1.call-start = ((), (), s32[]{:S(2)}) async-start(), calls=%async_computation.1 | async-start | bytes 4423680 | tf_op jit(solution)/shard_map/all_gather | solution.py:138
  9.7 4.5 %copy-start.12 = (f32[6,2,2,32]{3,2,1,0:T(2,128)S(1)}, f32[6,2,2,32]{3,2,1,0:T(2,128)}, u32[]{:S(2)}) copy-start(f32[6,2,2,32]{3,2,1,0:T(2,128)} %param.18) | copy-start | bytes 9220
  9.7 28.5 %copy-start.13 = (f32[1280]{0:T(1024)S(1)}, f32[1280]{0:T(1024)}, u32[]{:S(2)}) copy-start(f32[1280]{0:T(1024)} %param.19) | copy-start | bytes 15364
  9.7 28.5 %copy-start.14 = (f32[1280]{0:T(1024)S(1)}, f32[1280]{0:T(1024)}, u32[]{:S(2)}) copy-start(f32[1280]{0:T(1024)} %param.20) | copy-start | bytes 15364
  9.7 207.5 %all-gather.5.cloned.1.call-start = ((), (), s32[]{:S(2)}) async-start(), calls=%async_computation | async-start | bytes 4423680 | tf_op jit(solution)/shard_map/all_gather | solution.py:137
  12.0 274.5 %all-gather.9.cloned.1.call-start = ((), (), s32[]{:S(2)}) async-start(), calls=%async_computation.2 | async-start | bytes 4423680 | tf_op jit(solution)/shard_map/all_gather | solution.py:137
  38.2 3.9 copy-start.18
  41.0 1.6 copy-start.1
  42.6 2.4 copy-start.19
  286.6 2.3 copy-start.2
  286.6 2.3 copy-start.11
  288.9 2.1 copy-start.8
  315.6 0.8 copy-start.4
  318.4 1.2 copy-start.3
  319.6 2.1 copy-start.9
  321.7 1.0 copy-start.10
  347.4 0.8 copy-start.6
  348.2 6.8 %copy-start.15 = (f32[1280]{0:T(1024)S(1)}, f32[1280]{0:T(1024)}, u32[]{:S(2)}) copy-start(f32[1280]{0:T(1024)} %param.24) | copy-start | bytes 15364
  348.2 6.8 %copy-start.16 = (f32[1280]{0:T(1024)S(1)}, f32[1280]{0:T(1024)}, u32[]{:S(2)}) copy-start(f32[1280]{0:T(1024)} %param.25) | copy-start | bytes 15364
  352.2 2.8 copy-start.5
  352.2 2.8 copy-start.7
  355.6 10.8 %collective-permute-start = (bf16[1,64,1280]{2,1,0:T(8,128)(2,1)S(1)}, bf16[1,64,1280]{2,1,0:T(8,128)(2,1)S(1)}, u32[]{:S(2)}, u32[]{:S(2)}) collective-permute-start(bf16[1,64,1280]{2,1,0:T(8,128)(2,1)S(1)} %get-tuple-element.15), channel_id=1, source_target_pairs={{0,1},{1,2},{2,3},{3,4},{4,5},{5,6},{6,7},{8,9},{9,10},{10,11},{11... | collective-permute-start | bytes 491528 | tf_op jit(solution)/shard_map/ppermute | solution.py:29
  357.8 10.1 %collective-permute-start.1 = (bf16[1,64,1280]{2,1,0:T(8,128)(2,1)S(1)}, bf16[1,64,1280]{2,1,0:T(8,128)(2,1)S(1)}, u32[]{:S(2)}, u32[]{:S(2)}) collective-permute-start(bf16[1,64,1280]{2,1,0:T(8,128)(2,1)S(1)} %get-tuple-element.16), channel_id=1, source_target_pairs={{1,0},{2,1},{3,2},{4,3},{5,4},{6,5},{7,6},{9,8},{10,9},{11,10},{12... | collective-permute-start | bytes 491528 | tf_op jit(solution)/shard_map/ppermute | solution.py:31
  369.4 0.7 copy-start.20
  386.0 0.7 copy-start.17
Sparse Core Ops, SparseCore 0:
  9.7 68.4 all-gather.10
  80.5 67.1 all-gather.6
  150.0 67.1 all-gather.4
  219.4 67.1 all-gather.8
